TPU v7x, 512 devices: a whole 4x8x8 slice. The times are simulated.
512 devices in a mesh: row: 64 (over x, y, core), col: 8 (over z).
Axes of the slice: x: 4, y: 8, z: 8, core: 2. Of those that a mesh axis runs over, the one named last changes fastest.
Arguments:
- grad_out: bfloat16 [2048, 12288], P('row', 'col'), may hold values from -3.5 to 3.5
- pre_act: bfloat16 [2048, 24576], P('col', 'row'), may hold values from -6 to 6
- down_weight: bfloat16 [24576, 12288], P('row', 'col'), may hold values from -0.0546875 to 0.0546875
Outputs:
- grad_pre: bfloat16 [2048, 24576], P('col', 'row')
- grad_weight: bfloat16 [24576, 12288], P('row', 'col')
All inputs are finite; a program needn't handle non-finite values.
Results may differ from a plain program's by a relative error of at most 0.015.
Values may be sent and summed in bfloat16 or wider, within the bound.
No kernel may reach another device: no remote copies, remote signals or barrier semaphores. Data moves between devices by JAX's collectives and lax.ppermute only.
A program may use at most 64 MiB of HBM per device.

v0:
```python
import jax
import jax.numpy as jnp
from jax import lax
from jax.sharding import PartitionSpec as P

coef = 0.7978845608
cubic = 0.044715


def gelu_fwd(x):
    return 0.5 * x * (1.0 + jnp.tanh(coef * (x + cubic * x * x * x)))


def gelu_grad(x):
    inner = coef * (x + cubic * x * x * x)
    tangent = jnp.tanh(inner)
    return 0.5 * (1.0 + tangent) + 0.5 * x * (1.0 - tangent * tangent) * coef * (
        1.0 + 3.0 * cubic * x * x
    )


def body(grad_out, pre_act, down_weight):
    grad_all = lax.all_gather(grad_out, "row", axis=0, tiled=True)
    pre_all = lax.all_gather(pre_act, "col", axis=0, tiled=True)
    hidden = gelu_fwd(pre_all.astype(jnp.float32)).astype(jnp.bfloat16)
    grad_weight = lax.dot_general(
        hidden, grad_all, (((0,), (0,)), ((), ())), preferred_element_type=jnp.float32
    ).astype(jnp.bfloat16)
    partial_term = lax.dot_general(
        grad_all, down_weight, (((1,), (1,)), ((), ())), preferred_element_type=jnp.float32
    )
    grad_hidden = lax.psum_scatter(
        partial_term.astype(jnp.bfloat16), "col", scatter_dimension=0, tiled=True
    ).astype(jnp.float32)
    grad_pre = (grad_hidden * gelu_grad(pre_act.astype(jnp.float32))).astype(jnp.bfloat16)
    return (grad_pre, grad_weight)


def solution(mesh):
    in_specs = (P("row", "col"), P("col", "row"), P("row", "col"))
    out_specs = (P("col", "row"), P("row", "col"))
    return jax.shard_map(body, mesh=mesh, in_specs=in_specs, out_specs=out_specs, check_vma=False)
```

profile of v0, /device:TPU:2, one launch (start us, length us, event | category | flops | bytes accessed | tf_op | source)
XLA Modules:
  0.0 197.5 jit_solution(17193629523569997921)
XLA Ops:
  7.2 0.0 copy-start
  7.2 0.0 all-gather.3.cloned.1.call-start
  7.2 0.7 all-gather.3.cloned.1.call-update
  7.9 0.0 all-gather.5.cloned.1.call-start
  8.0 0.7 all-gather.5.cloned.1.call-update
  8.7 0.0 reduce-scatter.2.cloned.1.call-start
  8.7 91.8 %all-gather.3.cloned.1.call-done = bf16[2048,1536]{1,0:T(8,128)(2,1)} async-done(((bf16[32,1536]{1,0:T(8,128)(2,1)}), bf16[2048,1536]{1,0:T(8,128)(2,1)}) %all-gather.3.cloned.1.call-update) | async-done | bytes 6291472 | tf_op jit(solution)/shard_map/all_gather | solution.py:23
  100.5 0.0 copy-done
  100.5 7.5 %convolution_convert_fusion.1 = bf16[2048,384]{1,0:T(8,128)(2,1)} fusion(bf16[2048,1536]{1,0:T(8,128)(2,1)} %all-gather.3.cloned.1.call-done, bf16[384,1536]{1,0:T(8,128)(2,1)S(1)} %copy-done), kind=kOutput, calls=%fused_computation.11 | convolution fusion | flops 2416705536 | bytes 9043968 | tf_op jit(solution)/shard_map/dot_general | solution.py:29
  108.0 0.0 reduce-scatter.2.cloned.1.call-update
  108.0 0.0 copy-start.1
  108.0 35.9 %all-gather.5.cloned.1.call-done = bf16[2048,384]{1,0:T(8,128)(2,1)} async-done(((bf16[256,384]{1,0:T(8,128)(2,1)}), bf16[2048,384]{1,0:T(8,128)(2,1)}) %all-gather.5.cloned.1.call-update) | async-done | bytes 1572880 | tf_op jit(solution)/shard_map/all_gather | solution.py:24
  143.9 7.0 %convolution_convert_fusion = bf16[384,1536]{1,0:T(8,128)(2,1)} fusion(bf16[2048,1536]{1,0:T(8,128)(2,1)} %all-gather.3.cloned.1.call-done, bf16[2048,384]{1,0:T(8,128)(2,1)} %all-gather.5.cloned.1.call-done), kind=kOutput, calls=%fused_computation.10 | convolution fusion | flops 2424373248 | bytes 9043968 | tf_op jit(solution)/shard_map/dot_general | solution.py:26
  150.9 38.2 %reduce-scatter.2.cloned.1.call-done = bf16[256,384]{1,0:T(8,128)(2,1)} async-done(((bf16[2048,384]{1,0:T(8,128)(2,1)}), bf16[256,384]{1,0:T(8,128)(2,1)}) %reduce-scatter.2.cloned.1.call-update) | async-done | bytes 196624 | tf_op jit(solution)/shard_map/reduce_scatter | solution.py:32
  189.1 0.0 copy-done.1
  189.1 1.9 fusion.17
Async XLA Ops:
  7.2 93.3 %copy-start = (bf16[384,1536]{1,0:T(8,128)(2,1)S(1)}, bf16[384,1536]{1,0:T(8,128)(2,1)}, u32[]{:S(2)}) copy-start(bf16[384,1536]{1,0:T(8,128)(2,1)} %param.5) | copy-start | bytes 3538948
  7.2 93.3 %all-gather.3.cloned.1.call-start = ((), (), s32[]{:S(2)}) async-start(), calls=%async_computation.1 | async-start | bytes 6389760 | tf_op jit(solution)/shard_map/all_gather | solution.py:23
  7.9 136.0 %all-gather.5.cloned.1.call-start = ((), (), s32[]{:S(2)}) async-start(), calls=%async_computation.3 | async-start | bytes 1769472 | tf_op jit(solution)/shard_map/all_gather | solution.py:24
  8.7 180.4 %reduce-scatter.2.cloned.1.call-start = ((), (), s32[]{:S(2)}) async-start(), calls=%async_computation.2 | async-start | bytes 1769472 | tf_op jit(solution)/shard_map/reduce_scatter | solution.py:32
  108.0 81.1 %copy-start.1 = (bf16[256,384]{1,0:T(8,128)(2,1)S(1)}, bf16[256,384]{1,0:T(8,128)(2,1)}, u32[]{:S(2)}) copy-start(bf16[256,384]{1,0:T(8,128)(2,1)} %param.4) | copy-start | bytes 589828
Sparse Core Ops, SparseCore 0:
  11.3 89.1 all-gather.2
  102.6 41.3 all-gather.4
  146.8 42.2 reduce-scatter.1
where the time goes:
time: 198 us; the launch traced here: 197 us
  waiting for transfers between devices  167 us (84%)
  matrix products  14.5 us (7%)
  between operations  13.8 us (7%)
    all_gather x1, waiting for transfers between devices, body(): grad_all = lax.all_gather(grad_out, 'row', axis=0, tiled=True)  91.8 us
    reduce_scatter x1, waiting for transfers between devices, body(): lax.psum_scatter(partial_term.astype(jnp.bfloat16), 'col', scatter_dimens...  38.2 us
    all_gather x1, waiting for transfers between devices, body(): pre_all = lax.all_gather(pre_act, 'col', axis=0, tiled=True)  35.9 us
    dot_general x1, matrix products, body(): lax.dot_general(grad_all, down_weight, (((1,), (1,)), ((), ())), preferre...  7.48 us
    dot_general x1, matrix products, body(): lax.dot_general(hidden, grad_all, (((0,), (0,)), ((), ())), preferred_ele...  6.99 us
  transfers between devices with their start and end apart: 3, of which 3 were waited for; matrix products, arithmetic and copies ran while one was open for 7% of the time, Pallas kernels for 0%

commit v1 on v0

--- a/solution.py
+++ b/solution.py
@@ -21,7 +21,9 @@
 
 def body(grad_out, pre_act, down_weight):
     grad_all = lax.all_gather(grad_out, "row", axis=0, tiled=True)
-    pre_all = lax.all_gather(pre_act, "col", axis=0, tiled=True)
+    pre_all = jnp.concatenate(
+        lax.all_to_all(jnp.stack([pre_act] * lax.axis_size("col")), "col", 0, 0), axis=0
+    )
     hidden = gelu_fwd(pre_all.astype(jnp.float32)).astype(jnp.bfloat16)
     grad_weight = lax.dot_general(
         hidden, grad_all, (((0,), (0,)), ((), ())), preferred_element_type=jnp.float32

time: 198 us -> 160 us (0.81)
  the two profiles are of different devices: /device:TPU:2 before, /device:TPU:4 now
where the time goes in v1:
time: 160 us; the launch traced here: 159 us
  waiting for transfers between devices  117 us (73%)
  between operations  14.1 us (9%)
  matrix products  13.9 us (9%)
  starting transfers between devices  10.4 us (6%)
  local copies, waits for them, and re-layouts  2.31 us (1%)
  other arithmetic  1.89 us (1%)
    all_gather x1, waiting for transfers between devices, body(): grad_all = lax.all_gather(grad_out, 'row', axis=0, tiled=True)  79.8 us
    reduce_scatter x1, waiting for transfers between devices, body(): lax.psum_scatter(partial_term.astype(jnp.bfloat16), 'col', scatter_dimens...  36.3 us
    all_to_all x1, starting transfers between devices, body(): lax.all_to_all(jnp.stack([pre_act] * lax.axis_size('col')), 'col', 0, 0)  10.3 us
    dot_general x1, matrix products, body(): lax.dot_general(grad_all, down_weight, (((1,), (1,)), ((), ())), preferre...  7.38 us
    dot_general x1, matrix products, body(): lax.dot_general(hidden, grad_all, (((0,), (0,)), ((), ())), preferred_ele...  6.54 us
  transfers between devices with their start and end apart: 3, of which 2 were waited for; matrix products, arithmetic and copies ran while one was open for 10% of the time, Pallas kernels for 0%

profile of v1, /device:TPU:4, one launch (start us, length us, event | category | flops | bytes accessed | tf_op | source)
XLA Modules:
  0.0 159.3 jit_solution(14611837673106509766)
XLA Ops:
  7.2 0.0 copy-start
  7.2 0.0 all-gather.2.cloned.1.call-start
  7.2 0.7 all-gather.2.cloned.1.call-update
  7.9 2.3 %stack.2 = bf16[8,256,384]{2,1,0:T(8,128)(2,1)} broadcast(bf16[256,384]{1,0:T(8,128)(2,1)} %param.4), dimensions={1,2} | broadcast | bytes 1769472 | tf_op jit(solution)/shard_map/stack | solution.py:25
  10.2 10.3 %all-to-all-start = ((bf16[8,256,384]{2,1,0:T(8,128)(2,1)}), bf16[8,256,384]{2,1,0:T(8,128)(2,1)S(1)}, u32[]{:S(2)}, u32[]{:S(2)}) async-start(bf16[8,256,384]{2,1,0:T(8,128)(2,1)} %stack.2), calls=%async_computation.1 | async-start | bytes 3145728 | tf_op jit(solution)/shard_map/all_to_all | solution.py:25
  20.5 0.0 reduce-scatter.2.cloned.1.call-start
  20.6 79.8 %all-gather.2.cloned.1.call-done = bf16[2048,1536]{1,0:T(8,128)(2,1)} async-done(((bf16[32,1536]{1,0:T(8,128)(2,1)}), bf16[2048,1536]{1,0:T(8,128)(2,1)}) %all-gather.2.cloned.1.call-update) | async-done | bytes 6291472 | tf_op jit(solution)/shard_map/all_gather | solution.py:23
  100.3 0.0 copy-done
  100.3 7.4 %convolution_convert_fusion.1 = bf16[2048,384]{1,0:T(8,128)(2,1)} fusion(bf16[2048,1536]{1,0:T(8,128)(2,1)} %all-gather.2.cloned.1.call-done, bf16[384,1536]{1,0:T(8,128)(2,1)S(1)} %copy-done), kind=kOutput, calls=%fused_computation.11 | convolution fusion | flops 2416705536 | bytes 9043968 | tf_op jit(solution)/shard_map/dot_general | solution.py:31
  107.7 0.0 reduce-scatter.2.cloned.1.call-update
  107.7 0.0 all-to-all-done
  107.7 0.0 copy-start.1
  107.8 6.5 %convolution_convert_fusion = bf16[384,1536]{1,0:T(8,128)(2,1)} fusion(bf16[2048,1536]{1,0:T(8,128)(2,1)} %all-gather.2.cloned.1.call-done, bf16[2048,384]{1,0:T(8,128)(2,1)S(1)} %bitcast.5), kind=kOutput, calls=%fused_computation.10 | convolution fusion | flops 2424373248 | bytes 9043968 | tf_op jit(solution)/shard_map/dot_general | solution.py:28
  114.3 36.3 %reduce-scatter.2.cloned.1.call-done = bf16[256,384]{1,0:T(8,128)(2,1)} async-done(((bf16[2048,384]{1,0:T(8,128)(2,1)}), bf16[256,384]{1,0:T(8,128)(2,1)}) %reduce-scatter.2.cloned.1.call-update) | async-done | bytes 196624 | tf_op jit(solution)/shard_map/reduce_scatter | solution.py:34
  150.6 0.0 copy-done.1
  150.6 1.9 %fusion.17 = bf16[256,384]{1,0:T(8,128)(2,1)} fusion(bf16[256,384]{1,0:T(8,128)(2,1)S(1)} %copy-done.1, bf16[256,384]{1,0:T(8,128)(2,1)} %reduce-scatter.2.cloned.1.call-done), kind=kLoop, calls=%fused_computation.30 | loop fusion | flops 2064384 | bytes 589824 | tf_op jit(solution)/shard_map/convert_element_type | solution.py:37
Async XLA Ops:
  7.2 93.2 %copy-start = (bf16[384,1536]{1,0:T(8,128)(2,1)S(1)}, bf16[384,1536]{1,0:T(8,128)(2,1)}, u32[]{:S(2)}) copy-start(bf16[384,1536]{1,0:T(8,128)(2,1)} %param.5) | copy-start | bytes 3538948
  7.2 93.1 %all-gather.2.cloned.1.call-start = ((), (), s32[]{:S(2)}) async-start(), calls=%async_computation.2 | async-start | bytes 6389760 | tf_op jit(solution)/shard_map/all_gather | solution.py:23
  10.2 97.5 %all-to-all-start = ((bf16[8,256,384]{2,1,0:T(8,128)(2,1)}), bf16[8,256,384]{2,1,0:T(8,128)(2,1)S(1)}, u32[]{:S(2)}, u32[]{:S(2)}) async-start(bf16[8,256,384]{2,1,0:T(8,128)(2,1)} %stack.2), calls=%async_computation.1 | async-start | bytes 3145728 | tf_op jit(solution)/shard_map/all_to_all | solution.py:25
  20.5 130.1 %reduce-scatter.2.cloned.1.call-start = ((), (), s32[]{:S(2)}) async-start(), calls=%async_computation.3 | async-start | bytes 1769472 | tf_op jit(solution)/shard_map/reduce_scatter | solution.py:34
  107.7 42.8 %copy-start.1 = (bf16[256,384]{1,0:T(8,128)(2,1)S(1)}, bf16[256,384]{1,0:T(8,128)(2,1)}, u32[]{:S(2)}) copy-start(bf16[256,384]{1,0:T(8,128)(2,1)} %param.4) | copy-start | bytes 589828
Sparse Core Ops, SparseCore 0:
  11.3 88.9 all-gather.1
  107.9 42.6 reduce-scatter.1
